TPU v7x, 256 devices: a whole 4x4x8 slice. The times are simulated.
256 devices in a mesh: dp: 32 (over z, x_lo, core), factor: 8 (over y, x_hi).
Axes of the slice: x: 4 (x_hi: 2, x_lo: 2; x = x_hi * 2 + x_lo), y: 4, z: 8, core: 2. Of those that a mesh axis runs over, the one named last changes fastest.
Arguments:
- activations: bfloat16 [65536, 14336], P('dp', 'factor'), may hold values from -6 to 6
- out_grads: bfloat16 [65536, 4096], P('dp', 'factor'), may hold values from -6 to 6
- proj_in: bfloat16 [14336, 256], P('factor'), may hold values from -0.046875 to 0.046875
- proj_out: bfloat16 [4096, 256], P('factor'), may hold values from -0.09375 to 0.09375
- basis_in: bfloat16 [256, 256], replicated, may hold values from -0.375 to 0.375
- basis_out: bfloat16 [256, 256], replicated, may hold values from -0.375 to 0.375
- eigen_values: float32 [256, 256], P('factor'), may hold values from 0.01 to 10
- query_in: bfloat16 [256, 8, 256], P('dp'), may hold values from -3 to 3
- query_out: bfloat16 [256, 8, 256], P('dp'), may hold values from -3 to 3
- lengths: int32 [32, 16], P('dp'), may hold values from 1 to 256, 2048 in all within a row
- continues: int32 [32], replicated, may hold values from 0 to 1, as said below
- owners: int32 [512, 1], replicated, may hold values from 0 to 31; in each aligned block of 512 rows (0 to 511, 512 to 1023, ...) at most 32 rows name the same one
Outputs:
- influence: float32 [1024, 256], P('dp')
Inputs may be any that keep to these rules, and one draw needn't show every extreme that they name: `lengths`: each row sums to 2048. `continues`: the flags of sequences 0, 15, 16 and 30 are 1; the flag of the last sequence is not read. `owners`: no dp index owns more than 32 document numbers, and one owns exactly 32.
All inputs are finite; a program needn't handle non-finite values.
Results may differ from a plain program's by a relative error of at most 0.0027.
Values may be sent and summed in bfloat16 or wider, within the bound.
No kernel may reach another device: no remote copies, remote signals or barrier semaphores. Data moves between devices by JAX's collectives and lax.ppermute only.
A program may use at most 64 MiB of HBM per device.

v0:
```python
import jax
import jax.numpy as jnp
from jax import lax
from jax.sharding import PartitionSpec as P

OWN_CAP = 32
DAMPING = 0.1
EPSILON = 1e-06


def from_behind(block, axis, distance):
    devices = range(lax.axis_size(axis))
    route = [(i - distance, i) for i in devices if i - distance in devices]
    return lax.ppermute(block, axis, route)


def per_device(
    activations,
    out_grads,
    proj_in,
    proj_out,
    basis_in,
    basis_out,
    eigen_values,
    query_in,
    query_out,
    lengths,
    continues,
    owners,
):
    tokens_here = activations.shape[0]
    pieces = lengths.shape[1]
    rank_slice = eigen_values.shape[0]
    rank_in = basis_in.shape[0]
    factor_index = lax.axis_index("factor")
    data_index = lax.axis_index("dp")
    data_count = lax.axis_size("dp")
    highest = lax.Precision.HIGHEST
    in_part = jnp.dot(activations, proj_in, preferred_element_type=jnp.float32)
    out_part = jnp.dot(out_grads, proj_out, preferred_element_type=jnp.float32)
    basis_in_wide = basis_in.astype(jnp.float32)
    basis_out_wide = basis_out.astype(jnp.float32)
    rot_in = lax.psum(jnp.dot(in_part, basis_in_wide, precision=highest), "factor")
    rot_out_rows = lax.psum_scatter(
        lax.dot_general(basis_out_wide, out_part, (((0,), (1,)), ((), ())), precision=highest),
        "factor",
        scatter_dimension=0,
        tiled=True,
    )
    piece_lengths = lengths[0]
    piece_ends = jnp.cumsum(piece_lengths)
    piece_starts = piece_ends - piece_lengths
    position = jnp.arange(tokens_here, dtype=jnp.int32)[:, None]
    member = ((position >= piece_starts[None, :]) & (position < piece_ends[None, :])).astype(
        jnp.float32
    )
    stacked = (member[:, :, None] * rot_out_rows.T[:, None, :]).reshape(
        tokens_here, pieces * rank_slice
    )
    grad_rows = lax.dot_general(stacked, rot_in, (((0,), (0,)), ((), ())), precision=highest)
    grad_rows = grad_rows.reshape(pieces, rank_slice * rank_in)
    preceding = from_behind(grad_rows[pieces - 1].astype(jnp.bfloat16), "dp", 1).astype(jnp.float32)
    joined_next = jnp.where(data_index < data_count - 1, continues[data_index], 0).astype(
        jnp.float32
    )
    joined_prev = jnp.where(data_index > 0, continues[jnp.maximum(data_index - 1, 0)], 0).astype(
        jnp.float32
    )
    grad_rows = grad_rows.at[0].add(joined_prev * preceding)
    grad_rows = grad_rows.at[pieces - 1].multiply(1.0 - joined_next)
    scale = (1.0 / (eigen_values + DAMPING)).reshape(-1)
    self_part = jnp.sum(grad_rows * grad_rows * scale[None, :], axis=1)
    grad_low = grad_rows.astype(jnp.bfloat16)
    basis_cut = lax.dynamic_slice_in_dim(basis_out_wide, factor_index * rank_slice, rank_slice, 1)
    q_out = jnp.einsum("qtk,kl->qtl", query_out.astype(jnp.float32), basis_cut, precision=highest)
    q_in = jnp.einsum("qtk,kl->qtl", query_in.astype(jnp.float32), basis_in_wide, precision=highest)
    outer = jnp.einsum("qti,qtj->qij", q_out, q_in, precision=highest)
    part = lax.dot_general(
        grad_low,
        lax.all_gather(
            (outer.reshape(query_in.shape[0], rank_slice * rank_in) * scale[None, :]).astype(
                jnp.bfloat16
            ),
            "dp",
            axis=0,
            tiled=True,
        ),
        (((1,), (1,)), ((), ())),
        preferred_element_type=jnp.float32,
    )
    own_all = owners[:, 0]
    doc_count = own_all.shape[0]
    mine_ids = data_index * pieces + jnp.arange(pieces, dtype=jnp.int32)
    own_mine = lax.dynamic_slice_in_dim(own_all, data_index * pieces, pieces)
    earlier = (own_all[None, :] == own_mine[:, None]) & (
        jnp.arange(doc_count, dtype=jnp.int32)[None, :] < mine_ids[:, None]
    )
    rank_mine = jnp.sum(earlier.astype(jnp.int32), axis=1)
    slot_index = own_mine * OWN_CAP + rank_mine
    slot_rows = data_count * OWN_CAP
    placing = (jnp.arange(slot_rows, dtype=jnp.int32)[:, None] == slot_index[None, :]).astype(
        jnp.float32
    )
    raw_total, self_total = lax.psum((part, self_part), "factor")
    relative = raw_total / jnp.sqrt(self_total + EPSILON)[:, None]
    placed = jnp.dot(placing, relative, precision=highest)
    return lax.psum_scatter(placed, "dp", scatter_dimension=0, tiled=True)


def solution(mesh):
    placed = (
        P("dp", "factor"),
        P("dp", "factor"),
        P("factor", None),
        P("factor", None),
        P(),
        P(),
        P("factor", None),
        P("dp", None, None),
        P("dp", None, None),
        P("dp", None),
        P(),
        P(),
    )
    return jax.shard_map(
        per_device, mesh=mesh, in_specs=placed, out_specs=P("dp", None), check_vma=False
    )
```

profile of v0, /device:TPU:8, one launch (start us, length us, event | category | flops | bytes accessed | tf_op | source)
XLA Modules:
  0.0 394.8 jit_solution(14859609049050436812)
XLA Ops:
  7.4 0.0 copy-start
  7.4 0.0 reduce-scatter.7.cloned.1.call-start
  7.4 1.6 copy-done
  9.0 1.7 fusion.17
  10.6 0.0 copy-done.2
  10.6 2.4 convolution_bitcast_fusion
  13.1 2.9 copy.22
  16.0 0.0 reduce-scatter.7.cloned.1.call-update
  16.0 0.0 copy-start.1
  16.0 0.0 all-reduce.3.cloned.1.call-start
  16.1 1.1 copy-done.8
  17.2 5.3 %fusion.18 = f32[2048,256]{1,0:T(8,128)S(1)} fusion(bf16[2048,1792]{1,0:T(8,128)(2,1)} %param.16, bf16[1792,256]{1,0:T(8,128)(2,1)S(1)} %copy-done.8), kind=kOutput, calls=%fused_computation.39 | convolution fusion | flops 1879048192 | bytes 10354688 | tf_op jit(solution)/shard_map/dot_general | solution.py:39
  22.5 2.4 fusion.19
  24.9 0.0 copy-start.7
  24.9 0.0 copy-start.5
  24.9 0.0 all-reduce.3.cloned.1.call-update
  24.9 0.0 all-gather.2.cloned.1.call-start
  25.0 0.6 copy-done.4
  25.7 0.1 fusion.4
  25.8 0.2 convolution_bitcast_fusion.2
  26.0 0.5 convolution_bitcast_fusion.1
  26.5 0.2 copy.28
  26.7 0.7 multiply_convert_fusion
  27.4 0.0 all-gather.2.cloned.1.call-update
  27.4 0.0 reduce-scatter.5.cloned.1.call-start
  27.5 0.7 fusion.16
  28.8 0.1 copy.19
  28.9 0.1 reduce.4
  29.7 0.1 dynamic-slice_bitcast_fusion
  29.8 0.2 convert_reduce_fusion
  29.9 0.1 multiply_add_fusion.1
  30.0 0.1 fusion.7
  30.1 70.0 %reduce-scatter.7.cloned.1.call-done = f32[32,2048]{1,0:T(8,128)} async-done(((f32[256,2048]{1,0:T(8,128)}), f32[32,2048]{1,0:T(8,128)}) %reduce-scatter.7.cloned.1.call-update) | async-done | bytes 262160
  100.2 3.4 broadcast_multiply_fusion
  103.6 108.7 %all-reduce.3.cloned.1.call-done = f32[2048,256]{1,0:T(8,128)} async-done(((f32[2048,256]{1,0:T(8,128)}), f32[2048,256]{1,0:T(8,128)}) %all-reduce.3.cloned.1.call-update) | async-done | bytes 2097168 | tf_op jit(solution)/shard_map/psum | solution.py:43
  212.3 6.0 %fusion.20 = f32[512,256]{1,0:T(8,128)S(1)} fusion(f32[2048,512]{0,1:T(8,128)} %bitcast.57, f32[2048,256]{1,0:T(8,128)} %all-reduce.3.cloned.1.call-done), kind=kOutput, calls=%fused_computation.41 | convolution fusion | flops 3221225472 | bytes 6815744 | tf_op jit(solution)/shard_map/dot_general | solution.py:60
  218.3 1.6 collective-permute-start
  219.9 0.1 reshape.133
  220.1 0.7 collective-permute-done
  220.7 0.1 scatter-add.4
  220.9 0.2 scatter-mul.4
  221.1 0.2 multiply_reduce_fusion
  221.3 0.0 all-gather.2.cloned.1.call-done
  221.3 3.4 fusion.1
  224.7 38.6 %all-reduce = (f32[16,256]{1,0:T(8,128)S(1)}, f32[16]{0:T(128)S(1)}) all-reduce(f32[16,256]{1,0:T(8,128)S(1)} %fusion.1, f32[16]{0:T(128)S(1)} %multiply_reduce_fusion), channel_id=1, replica_groups=mesh['dp'=32,'factor'=8] {'factor'}, use_global_device_ids=true, to_apply=%region_4.5 | all-reduce | flops 4112 | bytes 32896 | tf_op jit(solution)/shard_map/psum | solution.py:104
  263.3 1.6 fusion
  264.9 0.0 reduce-scatter.5.cloned.1.call-update
  264.9 122.4 %reduce-scatter.5.cloned.1.call-done = f32[32,256]{1,0:T(8,128)} async-done(((f32[1024,256]{1,0:T(8,128)}), f32[32,256]{1,0:T(8,128)}) %reduce-scatter.5.cloned.1.call-update) | async-done | bytes 32784 | tf_op jit(solution)/shard_map/reduce_scatter | solution.py:107
  (24 shorter events, 0.2 us)
Async XLA Ops:
  7.4 1.6 copy-start
  7.4 3.3 copy-start.2
  7.4 92.8 %reduce-scatter.7.cloned.1.call-start = ((), (), s32[]{:S(2)}) async-start(), calls=%async_computation.5 | async-start | bytes 2359296
  16.0 1.2 copy-start.8
  16.0 6.5 %copy-start.1 = (bf16[256,256]{1,0:T(8,128)(2,1)S(1)}, bf16[256,256]{1,0:T(8,128)(2,1)}, u32[]{:S(2)}) copy-start(bf16[256,256]{1,0:T(8,128)(2,1)} %param.20) | copy-start | bytes 393220
  16.0 196.3 %all-reduce.3.cloned.1.call-start = ((), (), s32[]{:S(2)}) async-start(), calls=%async_computation.2 | async-start | bytes 4194304 | tf_op jit(solution)/shard_map/psum | solution.py:43
  24.9 0.8 copy-start.4
  24.9 0.8 copy-start.3
  24.9 1.0 copy-start.9
  24.9 2.6 copy-start.6
  24.9 3.9 copy-start.7
  24.9 4.8 %copy-start.5 = (s32[512,1]{0,1:T(1,128)S(1)}, s32[512,1]{0,1:T(1,128)}, u32[]{:S(2)}) copy-start(s32[512,1]{0,1:T(1,128)} %param.27) | copy-start | bytes 6148
  24.9 196.4 %all-gather.2.cloned.1.call-start = ((), (), s32[]{:S(2)}) async-start(), calls=%async_computation.3 | async-start | bytes 4325376 | tf_op jit(solution)/shard_map/all_gather | solution.py:80
  27.4 359.9 %reduce-scatter.5.cloned.1.call-start = ((), (), s32[]{:S(2)}) async-start(), calls=%async_computation.4 | async-start | bytes 1081344 | tf_op jit(solution)/shard_map/reduce_scatter | solution.py:107
  218.3 2.4 collective-permute-start
Sparse Core Ops, SparseCore 0:
  16.1 83.9 reduce-scatter.6
  102.8 109.3 all-reduce.2
Sparse Core Ops, SparseCore 1:
  27.5 70.0 all-gather.1
  265.0 122.3 reduce-scatter.4
where the time goes:
time: 395 us
  waiting for transfers between devices  302 us (76%)
  blocking collectives  38.6 us (10%)
  matrix products  23.6 us (6%)
  between operations  16.4 us (4%)
  local copies, waits for them, and re-layouts  7.7 us (2%)
  other arithmetic  4.88 us (1%)
    reduce_scatter x1, waiting for transfers between devices, per_device(): return lax.psum_scatter(placed, 'dp', scatter_dimension=0, tiled=True)  122 us
    psum x1, waiting for transfers between devices, per_device(): lax.psum(jnp.dot(in_part, basis_in_wide, precision=highest), 'factor')  109 us
    unnamed x5, waiting for transfers between devices  70.1 us
    psum x1, blocking collectives, per_device(): raw_total, self_total = lax.psum((part, self_part), 'factor')  38.6 us
  transfers between devices with their start and end apart: 5, of which 4 were waited for; matrix products, arithmetic and copies ran while one was open for 5% of the time, Pallas kernels for 0%

commit v1 on v0

--- a/solution.py
+++ b/solution.py
@@ -40,7 +40,9 @@
     out_part = jnp.dot(out_grads, proj_out, preferred_element_type=jnp.float32)
     basis_in_wide = basis_in.astype(jnp.float32)
     basis_out_wide = basis_out.astype(jnp.float32)
-    rot_in = lax.psum(jnp.dot(in_part, basis_in_wide, precision=highest), "factor")
+    rot_in = jnp.sum(
+        lax.all_gather(jnp.dot(in_part, basis_in_wide, precision=highest), "factor"), axis=0
+    )
     rot_out_rows = lax.psum_scatter(
         lax.dot_general(basis_out_wide, out_part, (((0,), (1,)), ((), ())), precision=highest),
         "factor",

time: 395 us -> 522 us (1.32)
  waiting for transfers between devices: 302 us -> 421 us
  other arithmetic: 4.88 us -> 13.4 us
    all_gather x0 -> x1, waiting for transfers between devices: none -> 185 us  [per_device(): lax.all_gather(jnp.dot(in_part, basis_in_wide, precision=highest), 'factor')]
    psum x1 -> x0, waiting for transfers between devices: 109 us -> none  [per_device(): lax.psum(jnp.dot(in_part, basis_in_wide, precision=highest), 'factor')]
    all_gather x1, waiting for transfers between devices: 0.02 us -> 50.2 us  [per_device(): lax.all_gather((outer.reshape(query_in.shape[0], rank_slice * rank_in) *...]
    reduce_sum x0 -> x1, other arithmetic: none -> 8.51 us  [per_device(): jnp.sum(lax.all_gather(jnp.dot(in_part, basis_in_wide, precision=highest)...]
    reduce_scatter x1, waiting for transfers between devices: 122 us -> 116 us  [per_device(): return lax.psum_scatter(placed, 'dp', scatter_dimension=0, tiled=True)]
  transfers between devices with their start and end apart: 5 -> 5, of which waited for: 4 -> 5; matrix products, arithmetic and copies ran while one was open for 5% -> 6% of each run, Pallas kernels for 0% -> 0%
where the time goes in v1:
time: 522 us
  waiting for transfers between devices  421 us (81%)
  blocking collectives  39.5 us (8%)
  matrix products  23.6 us (5%)
  between operations  14.7 us (3%)
  other arithmetic  13.4 us (3%)
  local copies, waits for them, and re-layouts  7.66 us (1%)
    all_gather x1, waiting for transfers between devices, per_device(): lax.all_gather(jnp.dot(in_part, basis_in_wide, precision=highest), 'factor')  185 us
    reduce_scatter x1, waiting for transfers between devices, per_device(): return lax.psum_scatter(placed, 'dp', scatter_dimension=0, tiled=True)  116 us
    unnamed x5, waiting for transfers between devices  69.7 us
    all_gather x1, waiting for transfers between devices, per_device(): lax.all_gather((outer.reshape(query_in.shape[0], rank_slice * rank_in) *...  50.2 us
    psum x1, blocking collectives, per_device(): raw_total, self_total = lax.psum((part, self_part), 'factor')  39.5 us
  transfers between devices with their start and end apart: 5, of which 5 were waited for; matrix products, arithmetic and copies ran while one was open for 6% of the time, Pallas kernels for 0%

profile of v1, /device:TPU:8, one launch (start us, length us, event | category | flops | bytes accessed | tf_op | source)
XLA Modules:
  0.0 521.6 jit_solution(9944237145468364478)
XLA Ops:
  6.5 0.0 copy-start
  6.5 1.6 copy-done
  8.1 1.7 fusion.17
  9.8 2.4 convolution_bitcast_fusion
  12.2 2.9 copy.22
  15.1 0.0 reduce-scatter.7.cloned.1.call-update
  15.2 0.0 copy-start.1
  15.2 0.0 all-gather.6.cloned.1.call-start
  15.2 1.1 copy-done.8
  16.3 5.3 %fusion.18 = f32[2048,256]{1,0:T(8,128)S(1)} fusion(bf16[2048,1792]{1,0:T(8,128)(2,1)} %param.16, bf16[1792,256]{1,0:T(8,128)(2,1)S(1)} %copy-done.8), kind=kOutput, calls=%fused_computation.39 | convolution fusion | flops 1879048192 | bytes 10354688 | tf_op jit(solution)/shard_map/dot_general | solution.py:39
  21.6 2.5 fusion.19
  24.1 0.0 copy-start.7
  24.1 0.0 copy-start.5
  24.1 0.0 all-gather.6.cloned.1.call-update
  24.1 0.0 all-gather.4.cloned.1.call-start
  24.2 0.6 copy-done.4
  24.9 0.2 convolution_bitcast_fusion.2
  25.1 0.1 fusion.4
  25.3 0.5 convolution_bitcast_fusion.1
  25.7 0.2 copy.28
  25.9 0.7 multiply_convert_fusion
  26.6 0.0 all-gather.4.cloned.1.call-update
  26.6 0.0 reduce-scatter.5.cloned.1.call-start
  26.7 0.0 copy-done.6
  26.7 0.6 fusion.16
  27.9 0.1 copy.19
  28.1 0.1 reduce.4
  28.9 0.1 dynamic-slice_bitcast_fusion
  28.9 0.2 convert_reduce_fusion
  29.1 0.1 multiply_add_fusion.1
  29.2 0.1 fusion.7
  29.3 69.7 %reduce-scatter.7.cloned.1.call-done = f32[32,2048]{1,0:T(8,128)} async-done(((f32[256,2048]{1,0:T(8,128)}), f32[32,2048]{1,0:T(8,128)}) %reduce-scatter.7.cloned.1.call-update) | async-done | bytes 262160
  99.0 3.4 broadcast_multiply_fusion
  102.4 184.6 %all-gather.6.cloned.1.call-done = f32[16384,256]{1,0:T(8,128)} async-done(((f32[2048,256]{1,0:T(8,128)}), f32[16384,256]{1,0:T(8,128)}) %all-gather.6.cloned.1.call-update) | async-done | bytes 16777232 | tf_op jit(solution)/shard_map/all_gather | solution.py:44
  287.0 8.5 %reduce_sum.28 = f32[2048,256]{1,0:T(8,128)} reduce(f32[8,2048,256]{2,1,0:T(8,128)} %bitcast.58, f32[]{:T(128)} %constant.85.clone.1), dimensions={0}, to_apply=%region_3.4 | reduce | flops 3670016 | bytes 18874372 | tf_op jit(solution)/shard_map/reduce_sum | solution.py:43
  295.5 6.0 %fusion.20 = f32[512,256]{1,0:T(8,128)S(1)} fusion(f32[2048,512]{0,1:T(8,128)} %bitcast.59, f32[2048,256]{1,0:T(8,128)} %reduce_sum.28), kind=kOutput, calls=%fused_computation.41 | convolution fusion | flops 3221225472 | bytes 6815744 | tf_op jit(solution)/shard_map/dot_general | solution.py:62
  301.5 1.3 collective-permute-start
  302.8 0.1 reshape.133
  303.0 0.7 collective-permute-done
  303.7 0.1 scatter-add.4
  303.9 0.2 scatter-mul.4
  304.0 0.2 multiply_reduce_fusion
  304.2 50.2 %all-gather.4.cloned.1.call-done = bf16[256,8192]{1,0:T(8,128)(2,1)} async-done(((bf16[8,8192]{1,0:T(8,128)(2,1)}), bf16[256,8192]{1,0:T(8,128)(2,1)}) %all-gather.4.cloned.1.call-update) | async-done | bytes 4194320 | tf_op jit(solution)/shard_map/all_gather | solution.py:82
  354.4 3.4 fusion.1
  357.7 39.5 %all-reduce = (f32[16,256]{1,0:T(8,128)S(1)}, f32[16]{0:T(128)S(1)}) all-reduce(f32[16,256]{1,0:T(8,128)S(1)} %fusion.1, f32[16]{0:T(128)S(1)} %multiply_reduce_fusion), channel_id=1, replica_groups=mesh['dp'=32,'factor'=8] {'factor'}, use_global_device_ids=true, to_apply=%region_4.5 | all-reduce | flops 4112 | bytes 32896 | tf_op jit(solution)/shard_map/psum | solution.py:106
  397.3 1.6 fusion
  398.9 0.0 reduce-scatter.5.cloned.1.call-update
  398.9 116.2 %reduce-scatter.5.cloned.1.call-done = f32[32,256]{1,0:T(8,128)} async-done(((f32[1024,256]{1,0:T(8,128)}), f32[32,256]{1,0:T(8,128)}) %reduce-scatter.5.cloned.1.call-update) | async-done | bytes 32784 | tf_op jit(solution)/shard_map/reduce_scatter | solution.py:109
  (25 shorter events, 0.2 us)
Async XLA Ops:
  6.5 1.6 copy-start
  6.5 3.3 copy-start.2
  6.5 92.4 %reduce-scatter.7.cloned.1.call-start = ((), (), s32[]{:S(2)}) async-start(), calls=%async_computation.5 | async-start | bytes 2359296
  15.1 1.2 copy-start.8
  15.2 6.4 %copy-start.1 = (bf16[256,256]{1,0:T(8,128)(2,1)S(1)}, bf16[256,256]{1,0:T(8,128)(2,1)}, u32[]{:S(2)}) copy-start(bf16[256,256]{1,0:T(8,128)(2,1)} %param.20) | copy-start | bytes 393220
  15.2 271.8 %all-gather.6.cloned.1.call-start = ((), (), s32[]{:S(2)}) async-start(), calls=%async_computation.4 | async-start | bytes 18874368 | tf_op jit(solution)/shard_map/all_gather | solution.py:44
  24.1 0.8 copy-start.4
  24.1 0.8 copy-start.9
  24.1 1.0 copy-start.3
  24.1 2.6 copy-start.6
  24.1 3.8 copy-start.7
  24.1 4.7 copy-start.5
  24.1 330.2 %all-gather.4.cloned.1.call-start = ((), (), s32[]{:S(2)}) async-start(), calls=%async_computation.2 | async-start | bytes 4325376 | tf_op jit(solution)/shard_map/all_gather | solution.py:82
  26.6 488.5 %reduce-scatter.5.cloned.1.call-start = ((), (), s32[]{:S(2)}) async-start(), calls=%async_computation.3 | async-start | bytes 1081344 | tf_op jit(solution)/shard_map/reduce_scatter | solution.py:109
  301.5 2.1 collective-permute-start
Sparse Core Ops, SparseCore 0:
  15.3 83.6 reduce-scatter.6
  101.6 185.3 all-gather.5
  288.8 65.4 all-gather.3
  399.0 116.0 reduce-scatter.4
